TPU v7x, 512 devices: a whole 4x4x16 slice. The times are simulated.
512 devices in a mesh: seq: 16 (over z), exp: 32 (over x, y, core).
Axes of the slice: x: 4, y: 4, z: 16, core: 2. Of those that a mesh axis runs over, the one named last changes fastest.
Arguments:
- queries: bfloat16 [2048, 8192], P('seq', 'exp'), may hold values from -6 to 6
- key_matrix: bfloat16 [2048, 8192], P('seq', 'exp'), may hold values from -6 to 6
- values: bfloat16 [2048, 8192], P('seq', 'exp'), may hold values from -6 to 6
- log_decay: float32 [64, 2048], P('exp', 'seq'), may hold values from -3 to 0
- residual: bfloat16 [2048, 3072], P('seq'), may hold values from -6 to 6
- out_weight: bfloat16 [3072, 8192], P('seq', 'exp'), may hold values from -0.0625 to 0.0625
- router: bfloat16 [3072, 32], replicated, may hold values from -0.109375 to 0.109375
- expert_ids: int32 [2048, 2], P('seq'), may hold values from 0 to 31, all different within a row; in each aligned block of 128 rows (0 to 127, 128 to 255, ...) at most 12 rows name the same one
- up_weight: bfloat16 [32, 3072, 4608], P('exp', None, 'seq'), may hold values from -0.109375 to 0.109375
- down_weight: bfloat16 [32, 4608, 3072], P('exp', 'seq'), may hold values from -0.09375 to 0.09375
Outputs:
- layer_out: bfloat16 [2048, 3072], P(('seq', 'exp'))
Inputs may be any that keep to these rules, and one draw needn't show every extreme that they name: `expert_ids`: in each aligned block of 128 rows (one sequence block) no expert is named by more than 12 rows, a bound that some block reaches; a row names 2 different experts.
All inputs are finite; a program needn't handle non-finite values.
Results may differ from a plain program's by a relative error of at most 0.015.
Values may be sent and summed in bfloat16 or wider, within the bound.
No kernel may reach another device: no remote copies, remote signals or barrier semaphores. Data moves between devices by JAX's collectives and lax.ppermute only.
A program may use at most 64 MiB of HBM per device.

v0:
```python
import jax
import jax.numpy as jnp
from jax import lax
from jax.sharding import PartitionSpec as P


def prefix(x, axis, combine, identity):
    length, index = (lax.axis_size(axis), lax.axis_index(axis))
    everything = jax.tree.map(
        lambda part, kind: lax.all_gather(part.astype(kind), axis), x, (jnp.bfloat16, jnp.bfloat16)
    )
    start = jax.tree.map(
        lambda part, zero: jnp.broadcast_to(jnp.asarray(zero, part.dtype), part.shape), x, identity
    )

    def turn(k, before):
        reached = k < index
        new = combine(
            before, jax.tree.map(lambda part, own: part[k].astype(own.dtype), everything, x)
        )
        return jax.tree.map(lambda a, b: jnp.where(reached, a, b), new, before)

    return lax.fori_loop(0, length, turn, start)


def compose(earlier, later):
    return (earlier[0] * later[0], later[0][:, None, None] * earlier[1] + later[1])


def shards(
    queries,
    key_matrix,
    values,
    log_decay,
    residual,
    out_weight,
    router,
    expert_ids,
    up_weight,
    down_weight,
):
    rows = queries.shape[0]
    heads_here = log_decay.shape[0]
    width = queries.shape[1] // heads_here

    def split_heads(array):
        return array.astype(jnp.float32).reshape(rows, heads_here, width).transpose(1, 0, 2)

    qloc = split_heads(queries)
    kloc = split_heads(key_matrix)
    vloc = split_heads(values)
    cum = jnp.cumsum(log_decay, axis=1)
    last = cum[:, -1:]
    carry_decay = jnp.exp(last[:, 0])
    kscaled = kloc * jnp.exp(last - cum)[:, :, None]
    local_state = jnp.einsum("hjd,hje->hde", kscaled, vloc, precision=lax.Precision.HIGHEST)
    empty = jnp.zeros((heads_here, width, width), jnp.float32)
    _, state_in = prefix(
        (carry_decay, local_state), "seq", compose, (jnp.ones_like(carry_decay), empty)
    )
    lower = jnp.arange(rows)[:, None] >= jnp.arange(rows)[None, :]
    diff = cum[:, :, None] - cum[:, None, :]
    weight = jnp.where(lower[None], jnp.exp(jnp.where(lower[None], diff, 0.0)), 0.0)
    scores = jnp.einsum("hid,hjd->hij", qloc, kloc, precision=lax.Precision.HIGHEST) * weight
    inner = jnp.einsum("hij,hjd->hid", scores, vloc, precision=lax.Precision.HIGHEST)
    outer = jnp.exp(cum)[:, :, None] * jnp.einsum(
        "hid,hde->hie", qloc, state_in, precision=lax.Precision.HIGHEST
    )
    mixed = inner + outer
    mixed = mixed * lax.rsqrt(jnp.mean(mixed * mixed, axis=-1, keepdims=True) + 1e-06)
    attn = mixed.transpose(1, 0, 2).reshape(rows, heads_here * width).astype(jnp.bfloat16)
    stream = residual.astype(jnp.float32)
    normed = (stream * lax.rsqrt(jnp.mean(stream * stream, axis=-1, keepdims=True) + 1e-05)).astype(
        jnp.bfloat16
    )
    logits = jnp.dot(normed, router, preferred_element_type=jnp.float32)
    count_experts = router.shape[1]
    select_experts = (
        expert_ids[:, :, None] == jnp.arange(count_experts, dtype=jnp.int32)[None, None, :]
    )
    chosen = jnp.sum(jnp.where(select_experts, logits[:, None, :], 0.0), axis=-1)
    score = jax.nn.sigmoid(chosen)
    gates = score / jnp.sum(score, axis=1, keepdims=True)
    topk = expert_ids.shape[1]
    owner = lax.axis_index("exp")
    capacity = 3 * rows * topk // (2 * lax.axis_size("exp"))
    mine = (expert_ids.reshape(-1) == owner).astype(jnp.int32)
    ranks = jnp.cumsum(mine) - mine
    slot_pick = (ranks[None, :] == jnp.arange(capacity, dtype=jnp.int32)[:, None]) & (
        mine[None, :] == 1
    )
    slot_pick = slot_pick.astype(jnp.float32).reshape(capacity, rows, topk)
    token_pick = jnp.sum(slot_pick, axis=2).astype(jnp.bfloat16)
    slot_rows = jnp.dot(token_pick, normed, preferred_element_type=jnp.float32).astype(jnp.bfloat16)
    gathered_rows, full_weight = (
        lax.all_gather(slot_rows, "seq", axis=0, tiled=True),
        lax.all_gather(out_weight, "seq", axis=0, tiled=True),
    )
    projected = lax.dot_general(
        attn, full_weight, (((1,), (1,)), ((), ())), preferred_element_type=jnp.float32
    )
    hidden = jax.nn.silu(
        jnp.dot(gathered_rows, up_weight[0], preferred_element_type=jnp.float32)
    ).astype(jnp.bfloat16)
    expert_out = lax.psum_scatter(
        jnp.dot(hidden, down_weight[0], preferred_element_type=jnp.float32).astype(jnp.bfloat16),
        "seq",
        scatter_dimension=0,
        tiled=True,
    ).astype(jnp.float32)
    combine = jnp.einsum("cbk,bk->bc", slot_pick, gates, precision=lax.Precision.HIGHEST)
    contribution = jnp.dot(combine, expert_out, precision=lax.Precision.HIGHEST)
    summed = lax.psum_scatter(
        (projected + contribution).astype(jnp.bfloat16), "exp", scatter_dimension=0, tiled=True
    ).astype(jnp.float32)
    own_rows = summed.shape[0]
    own = lax.dynamic_slice_in_dim(stream, owner * own_rows, own_rows, 0)
    return (own + summed).astype(jnp.bfloat16)


def solution(mesh):
    in_specs = (
        P("seq", "exp"),
        P("seq", "exp"),
        P("seq", "exp"),
        P("exp", "seq"),
        P("seq", None),
        P("seq", "exp"),
        P(),
        P("seq", None),
        P("exp", None, "seq"),
        P("exp", "seq", None),
    )
    out_specs = P(("seq", "exp"), None)
    return jax.shard_map(shards, mesh=mesh, in_specs=in_specs, out_specs=out_specs, check_vma=False)
```

profile of v0, /device:TPU:1, one launch (start us, length us, event | category | flops | bytes accessed | tf_op | source)
XLA Modules:
  0.0 382.8 jit_solution(2274321475533020910)
XLA Ops:
  6.6 1.2 reduce_window_sum.27
  9.0 1.7 convolution_convert_fusion.2
  12.6 1.4 multiply_reduce_fusion
  14.0 1.0 fusion.3
  17.5 30.4 %all-reduce = bf16[32]{0:T(256)(128)(2,1)S(1)} all-reduce(bf16[32]{0:T(256)(128)(2,1)S(1)} %dynamic-update-slice), channel_id=2, replica_groups=mesh['seq'=16,'exp'=32] {'seq'}, use_global_device_ids=true, to_apply=%add | all-reduce | flops 32 | bytes 128
  49.4 26.7 %all-gather.9.cloned.1.call-done = bf16[32,128,128]{2,1,0:T(8,128)(2,1)} async-done(((bf16[2,128,128]{2,1,0:T(8,128)(2,1)}), bf16[32,128,128]{2,1,0:T(8,128)(2,1)}) %all-gather.9.cloned.1.call-update) | async-done | bytes 1048592 | tf_op jit(solution)/shard_map/all_gather | solution.py:10
  76.1 15.5 %while.14 = (s32[]{:T(128)}, f32[2,128,128]{2,1,0:T(8,128)S(1)}, s32[]{:T(128)}, bf16[16,2]{1,0:T(8,128)(2,1)S(1)}, bf16[16,2,128,128]{3,2,1,0:T(8,128)(2,1)}, /*index=5*/s32[]{:T(128)}, s32[]{:T(128)}) while((s32[]{:T(128)}, f32[2,128,128]{2,1,0:T(8,128)S(1)}, s32[]{:T(128)}, bf16[16,2]{1,0:T(8,128)(2,1)S(1)}, ...), condition=%wide.region_2.3_spmd.clone, body=%wide.region_1.2_spmd.clone.sunk | while | flops 163846 | bytes 327805 | solution.py:23
  92.3 55.7 %all-gather.11.cloned.1.call-done = bf16[16,12,3072]{2,1,0:T(8,128)(2,1)} async-done(((bf16[1,12,3072]{2,1,0:T(8,128)(2,1)}), bf16[16,12,3072]{2,1,0:T(8,128)(2,1)}) %all-gather.11.cloned.1.call-update) | async-done | bytes 1179664 | tf_op jit(solution)/shard_map/all_gather | solution.py:96
  147.9 2.3 reshape.178
  150.2 4.7 %convolution_convert_fusion = bf16[192,3072]{1,0:T(8,128)(2,1)} fusion(bf16[1,288,3072]{2,1,0:T(8,128)(2,1)S(1)} %copy-done, bf16[192,3072]{1,0:T(8,128)(2,1)} %reshape.178, bf16[1,3072,288]{1,2,0:T(8,128)(2,1)} %param.20), kind=kOutput, calls=%fused_computation.3 | convolution fusion | flops 680343552 | bytes 5898240 | tf_op jit(solution)/shard_map/dot_general | solution.py:106
  154.9 35.1 %fusion = bf16[16,3072]{1,0:T(8,128)(2,1)S(1)} fusion(bf16[192,3072]{1,0:T(8,128)(2,1)} %convolution_convert_fusion), kind=kCustom, calls=%all-reduce-scatter | all-reduce-scatter fusion | flops 786433 | bytes 1280000
  190.1 1.3 collective-permute-start
  191.4 3.6 collective-permute-start.1
  195.0 4.1 %collective-permute-start.2 = (bf16[16,3072]{1,0:T(8,128)(2,1)S(1)}, bf16[16,3072]{1,0:T(8,128)(2,1)S(1)}, u32[]{:S(2)}, u32[]{:S(2)}) collective-permute-start(bf16[16,3072]{1,0:T(8,128)(2,1)S(1)} %fusion), channel_id=1, source_target_pairs={{0,96},{32,128},{64,160},{96,192},{128,224},{160,256},{192,288},{2... | collective-permute-start | bytes 294920
  199.2 3.1 collective-permute-start.3
  202.3 3.2 collective-permute-done.3
  206.2 1.9 concatenate
  208.1 16.1 %all-gather.7.cloned.1.call-done = bf16[3072,256]{1,0:T(8,128)(2,1)} async-done(((bf16[192,256]{1,0:T(8,128)(2,1)}), bf16[3072,256]{1,0:T(8,128)(2,1)}) %all-gather.7.cloned.1.call-update) | async-done | bytes 1572880 | tf_op jit(solution)/shard_map/all_gather | solution.py:97
  224.2 2.0 fusion.34
  226.3 1.8 fusion.2
  228.1 1.3 convert_element_type.97
  229.4 1.3 dynamic-slice.3
  231.3 143.4 %all-reduce.6.cloned.1.call-done = bf16[128,3072]{1,0:T(8,128)(2,1)} async-done(((bf16[128,3072]{1,0:T(8,128)(2,1)}), bf16[128,3072]{1,0:T(8,128)(2,1)}) %all-reduce.6.cloned.1.call-update) | async-done | bytes 786448
  374.7 1.5 add_convert_fusion
  (94 shorter events, 22.2 us)
Async XLA Ops:
  6.5 143.7 %copy-start = (bf16[1,288,3072]{2,1,0:T(8,128)(2,1)S(1)}, bf16[1,288,3072]{2,1,0:T(8,128)(2,1)}, u32[]{:S(2)}) copy-start(bf16[1,288,3072]{2,1,0:T(8,128)(2,1)} %param.21) | copy-start | bytes 5308420
  6.5 9.5 %copy-start.6 = (u32[512]{0:T(512)S(1)}, u32[512]{0:T(512)}, u32[]{:S(2)}) copy-start(u32[512]{0:T(512)} %constant.67) | copy-start | bytes 6148
  6.5 7.5 %copy-start.1 = (bf16[128,3072]{1,0:T(8,128)(2,1)S(1)}, bf16[128,3072]{1,0:T(8,128)(2,1)}, u32[]{:S(2)}) copy-start(bf16[128,3072]{1,0:T(8,128)(2,1)} %param.16) | copy-start | bytes 2359300
  6.5 41.4 %copy-start.7 = (bf16[3072,32]{0,1:T(8,128)(2,1)S(1)}, bf16[3072,32]{0,1:T(8,128)(2,1)}, u32[]{:S(2)}) copy-start(bf16[3072,32]{0,1:T(8,128)(2,1)} %param.18) | copy-start | bytes 589828
  6.5 69.6 %all-gather.9.cloned.1.call-start = ((), (), s32[]{:S(2)}) async-start(), calls=%async_computation.1 | async-start | bytes 1114112 | tf_op jit(solution)/shard_map/all_gather | solution.py:10
  10.7 137.3 %all-gather.11.cloned.1.call-start = ((), (), s32[]{:S(2)}) async-start(), calls=%async_computation.2 | async-start | bytes 1671168 | tf_op jit(solution)/shard_map/all_gather | solution.py:96
  12.2 36.2 %copy-start.5 = (s32[128,2]{0,1:T(2,128)S(1)}, s32[128,2]{0,1:T(2,128)}, u32[]{:S(2)}) copy-start(s32[128,2]{0,1:T(2,128)} %param.19) | copy-start | bytes 3076
  12.2 36.3 %copy-start.4 = (bf16[128,256]{1,0:T(8,128)(2,1)S(1)}, bf16[128,256]{1,0:T(8,128)(2,1)}, u32[]{:S(2)}) copy-start(bf16[128,256]{1,0:T(8,128)(2,1)} %param.12) | copy-start | bytes 196612
  15.0 209.2 %all-gather.7.cloned.1.call-start = ((), (), s32[]{:S(2)}) async-start(), calls=%async_computation | async-start | bytes 1671168 | tf_op jit(solution)/shard_map/all_gather | solution.py:97
  15.7 359.0 %all-reduce.6.cloned.1.call-start = ((), (), s32[]{:S(2)}) async-start(), calls=%async_computation.3 | async-start | bytes 1572864
  48.4 43.5 %copy-start.2 = (bf16[128,256]{1,0:T(8,128)(2,1)S(1)}, bf16[128,256]{1,0:T(8,128)(2,1)}, u32[]{:S(2)}) copy-start(bf16[128,256]{1,0:T(8,128)(2,1)} %param.14) | copy-start | bytes 196612
  190.1 15.4 %collective-permute-start = (bf16[16,3072]{1,0:T(8,128)(2,1)S(1)}, bf16[16,3072]{1,0:T(8,128)(2,1)S(1)}, u32[]{:S(2)}, u32[]{:S(2)}) collective-permute-start(bf16[16,3072]{1,0:T(8,128)(2,1)S(1)} %fusion), channel_id=1, source_target_pairs={{0,32},{32,64},{64,96},{96,128},{128,160},{160,192},{192,224},{224... | collective-permute-start | bytes 294920
  191.4 14.1 %collective-permute-start.1 = (bf16[16,3072]{1,0:T(8,128)(2,1)S(1)}, bf16[16,3072]{1,0:T(8,128)(2,1)S(1)}, u32[]{:S(2)}, u32[]{:S(2)}) collective-permute-start(bf16[16,3072]{1,0:T(8,128)(2,1)S(1)} %fusion), channel_id=1, source_target_pairs={{0,64},{32,96},{64,128},{96,160},{128,192},{160,224},{192,256},{22... | collective-permute-start | bytes 294920
  195.0 11.2 %collective-permute-start.2 = (bf16[16,3072]{1,0:T(8,128)(2,1)S(1)}, bf16[16,3072]{1,0:T(8,128)(2,1)S(1)}, u32[]{:S(2)}, u32[]{:S(2)}) collective-permute-start(bf16[16,3072]{1,0:T(8,128)(2,1)S(1)} %fusion), channel_id=1, source_target_pairs={{0,96},{32,128},{64,160},{96,192},{128,224},{160,256},{192,288},{2... | collective-permute-start | bytes 294920
  199.2 6.4 %collective-permute-start.3 = (bf16[12,3072]{1,0:T(8,128)(2,1)S(1)}, bf16[12,3072]{1,0:T(8,128)(2,1)S(1)}, u32[]{:S(2)}, u32[]{:S(2)}) collective-permute-start(bf16[12,3072]{1,0:T(8,128)(2,1)S(1)} %slice.16), channel_id=1, source_target_pairs={{0,128},{32,160},{64,192},{96,224},{128,256},{160,288},{192,320},{... | collective-permute-start | bytes 221192
  205.6 0.6 copy-start.3
Sparse Core Ops, SparseCore 0:
  10.8 65.3 all-gather.8
  78.2 69.6 all-gather.10
  150.0 74.1 all-gather.6
  228.2 146.4 all-reduce.5
where the time goes:
time: 384 us; the launch traced here: 383 us
  waiting for transfers between devices  246 us (64%)
  blocking collectives  65.5 us (17%)
  other arithmetic  21.9 us (6%)
  between operations  15.3 us (4%)
  matrix products  12.4 us (3%)
  starting transfers between devices  12.3 us (3%)
  local copies, waits for them, and re-layouts  9.14 us (2%)
    unnamed x9, waiting for transfers between devices  147 us
    unnamed x2, blocking collectives  65.5 us
    all_gather x1, waiting for transfers between devices, shards(): lax.all_gather(slot_rows, 'seq', axis=0, tiled=True)  55.7 us
    all_gather x1, waiting for transfers between devices, prefix(): lax.all_gather(part.astype(kind), axis)  26.7 us
    all_gather x1, waiting for transfers between devices, shards(): lax.all_gather(out_weight, 'seq', axis=0, tiled=True)  16.1 us
    select_n x16, other arithmetic, turn(): return jax.tree.map(lambda a, b: jnp.where(reached, a, b), new, before)  14.9 us
    unnamed x5, starting transfers between devices  12.2 us
  transfers between devices with their start and end apart: 8, of which 5 were waited for; matrix products, arithmetic and copies ran while one was open for 18% of the time, Pallas kernels for 0%

commit v1 on v0

--- a/solution.py
+++ b/solution.py
@@ -2,6 +2,11 @@
 import jax.numpy as jnp
 from jax import lax
 from jax.sharding import PartitionSpec as P
+
+
+def reach_sectors_now(target):
+    m_next = jnp.stack([target for _ in range(lax.axis_size("seq"))], 0)
+    return jnp.concatenate(lax.all_to_all(m_next, "seq", 0, 0), 0)
 
 
 def prefix(x, axis, combine, identity):
@@ -94,7 +99,7 @@
     slot_rows = jnp.dot(token_pick, normed, preferred_element_type=jnp.float32).astype(jnp.bfloat16)
     gathered_rows, full_weight = (
         lax.all_gather(slot_rows, "seq", axis=0, tiled=True),
-        lax.all_gather(out_weight, "seq", axis=0, tiled=True),
+        reach_sectors_now(out_weight),
     )
     projected = lax.dot_general(
         attn, full_weight, (((1,), (1,)), ((), ())), preferred_element_type=jnp.float32

time: 384 us -> 410 us (1.068)
  blocking collectives: 65.5 us -> 125 us
  waiting for transfers between devices: 246 us -> 195 us
  starting transfers between devices: 12.3 us -> 28.8 us
    unnamed x2, blocking collectives: 65.5 us -> 125 us
    all_gather x1, waiting for transfers between devices: 26.7 us -> 0.02 us  [prefix(): lax.all_gather(part.astype(kind), axis)]
    all_gather x1, waiting for transfers between devices: 55.7 us -> 35.4 us  [shards(): lax.all_gather(slot_rows, 'seq', axis=0, tiled=True)]
    all_gather x1 -> x0, waiting for transfers between devices: 16.1 us -> none  [shards(): lax.all_gather(out_weight, 'seq', axis=0, tiled=True)]
    all_to_all x0 -> x1, starting transfers between devices: none -> 15.9 us  [reach_sectors_now(): return jnp.concatenate(lax.all_to_all(m_next, 'seq', 0, 0), 0)]
    unnamed x9 -> x8, waiting for transfers between devices: 147 us -> 160 us
  transfers between devices with their start and end apart: 8 -> 8, of which waited for: 5 -> 3; matrix products, arithmetic and copies ran while one was open for 18% -> 16% of each run, Pallas kernels for 0% -> 0%
where the time goes in v1:
time: 410 us; the launch traced here: 409 us
  waiting for transfers between devices  195 us (48%)
  blocking collectives  125 us (30%)
  starting transfers between devices  28.8 us (7%)
  other arithmetic  20.1 us (5%)
  between operations  15.3 us (4%)
  matrix products  12.4 us (3%)
  local copies, waits for them, and re-layouts  11.3 us (3%)
    unnamed x8, waiting for transfers between devices  160 us
    unnamed x2, blocking collectives  125 us
    all_gather x1, waiting for transfers between devices, shards(): lax.all_gather(slot_rows, 'seq', axis=0, tiled=True)  35.4 us
    all_to_all x1, starting transfers between devices, reach_sectors_now(): return jnp.concatenate(lax.all_to_all(m_next, 'seq', 0, 0), 0)  15.9 us
    select_n x16, other arithmetic, turn(): return jax.tree.map(lambda a, b: jnp.where(reached, a, b), new, before)  14.9 us
    unnamed x5, starting transfers between devices  12.8 us
  transfers between devices with their start and end apart: 8, of which 3 were waited for; matrix products, arithmetic and copies ran while one was open for 16% of the time, Pallas kernels for 0%

profile of v1, /device:TPU:1, one launch (start us, length us, event | category | flops | bytes accessed | tf_op | source)
XLA Modules:
  0.0 408.5 jit_solution(419063894703008042)
XLA Ops:
  6.5 1.1 reduce_window_sum.27
  7.9 1.0 copy.68
  8.9 1.7 convolution_convert_fusion.2
  10.6 2.2 stack.2
  12.8 15.9 %all-to-all-start = ((bf16[16,192,256]{2,1,0:T(8,128)(2,1)}), bf16[16,192,256]{2,1,0:T(8,128)(2,1)}, u32[]{:S(2)}, u32[]{:S(2)}) async-start(bf16[16,192,256]{2,1,0:T(8,128)(2,1)} %stack.2), calls=%async_computation | async-start | bytes 3145728 | tf_op jit(solution)/shard_map/all_to_all | solution.py:9
  30.3 1.0 fusion.3
  33.0 92.9 %all-reduce = bf16[32]{0:T(256)(128)(2,1)S(1)} all-reduce(bf16[32]{0:T(256)(128)(2,1)S(1)} %dynamic-update-slice), channel_id=2, replica_groups=mesh['seq'=16,'exp'=32] {'seq'}, use_global_device_ids=true, to_apply=%add | all-reduce | flops 32 | bytes 128
  127.4 15.5 %while.14 = (s32[]{:T(128)}, f32[2,128,128]{2,1,0:T(8,128)S(1)}, s32[]{:T(128)}, bf16[16,2]{1,0:T(8,128)(2,1)S(1)}, bf16[16,2,128,128]{3,2,1,0:T(8,128)(2,1)}, /*index=5*/s32[]{:T(128)}, s32[]{:T(128)}) while((s32[]{:T(128)}, f32[2,128,128]{2,1,0:T(8,128)S(1)}, s32[]{:T(128)}, bf16[16,2]{1,0:T(8,128)(2,1)S(1)}, ...), condition=%wide.region_2.3_spmd.clone, body=%wide.region_1.2_spmd.clone.sunk | while | flops 163846 | bytes 327805 | solution.py:28
  143.5 35.4 %all-gather.8.cloned.1.call-done = bf16[16,12,3072]{2,1,0:T(8,128)(2,1)} async-done(((bf16[1,12,3072]{2,1,0:T(8,128)(2,1)}), bf16[16,12,3072]{2,1,0:T(8,128)(2,1)}) %all-gather.8.cloned.1.call-update) | async-done | bytes 1179664 | tf_op jit(solution)/shard_map/all_gather | solution.py:101
  179.0 2.3 reshape.184
  181.3 4.7 %convolution_convert_fusion = bf16[192,3072]{1,0:T(8,128)(2,1)} fusion(bf16[1,288,3072]{2,1,0:T(8,128)(2,1)S(1)} %copy-done, bf16[192,3072]{1,0:T(8,128)(2,1)} %reshape.184, bf16[1,3072,288]{1,2,0:T(8,128)(2,1)} %param.20), kind=kOutput, calls=%fused_computation.3 | convolution fusion | flops 680343552 | bytes 5898240 | tf_op jit(solution)/shard_map/dot_general | solution.py:111
  186.0 31.9 %fusion = bf16[16,3072]{1,0:T(8,128)(2,1)S(1)} fusion(bf16[192,3072]{1,0:T(8,128)(2,1)} %convolution_convert_fusion), kind=kCustom, calls=%all-reduce-scatter | all-reduce-scatter fusion | flops 786433 | bytes 1280000
  218.0 2.7 collective-permute-start
  220.6 2.1 collective-permute-start.1
  222.8 4.0 collective-permute-start.2
  226.8 4.0 collective-permute-start.3
  230.8 1.6 collective-permute-done.3
  233.0 1.9 concatenate
  235.0 2.1 fusion.34
  237.1 1.8 fusion.2
  238.9 1.3 convert_element_type.97
  240.2 1.3 dynamic-slice.3
  242.1 158.3 %all-reduce.6.cloned.1.call-done = bf16[128,3072]{1,0:T(8,128)(2,1)} async-done(((bf16[128,3072]{1,0:T(8,128)(2,1)}), bf16[128,3072]{1,0:T(8,128)(2,1)}) %all-reduce.6.cloned.1.call-update) | async-done | bytes 786448
  400.5 1.5 add_convert_fusion
  (94 shorter events, 20.1 us)
Async XLA Ops:
  6.5 174.8 %copy-start = (bf16[1,288,3072]{2,1,0:T(8,128)(2,1)S(1)}, bf16[1,288,3072]{2,1,0:T(8,128)(2,1)}, u32[]{:S(2)}) copy-start(bf16[1,288,3072]{2,1,0:T(8,128)(2,1)} %param.21) | copy-start | bytes 5308420
  6.5 120.8 %all-gather.6.cloned.1.call-start = ((), (), s32[]{:S(2)}) async-start(), calls=%async_computation.1 | async-start | bytes 1114112 | tf_op jit(solution)/shard_map/all_gather | solution.py:15
  12.8 16.0 %copy-start.5 = (s32[128,2]{0,1:T(2,128)S(1)}, s32[128,2]{0,1:T(2,128)}, u32[]{:S(2)}) copy-start(s32[128,2]{0,1:T(2,128)} %param.19) | copy-start | bytes 3076
  12.8 17.2 %copy-start.1 = (bf16[128,3072]{1,0:T(8,128)(2,1)S(1)}, bf16[128,3072]{1,0:T(8,128)(2,1)}, u32[]{:S(2)}) copy-start(bf16[128,3072]{1,0:T(8,128)(2,1)} %param.16) | copy-start | bytes 2359300
  12.8 222.2 %all-to-all-start = ((bf16[16,192,256]{2,1,0:T(8,128)(2,1)}), bf16[16,192,256]{2,1,0:T(8,128)(2,1)}, u32[]{:S(2)}, u32[]{:S(2)}) async-start(bf16[16,192,256]{2,1,0:T(8,128)(2,1)} %stack.2), calls=%async_computation | async-start | bytes 3145728 | tf_op jit(solution)/shard_map/all_to_all | solution.py:9
  28.7 2.9 copy-start.6
  28.7 97.3 %copy-start.7 = (bf16[3072,32]{0,1:T(8,128)(2,1)S(1)}, bf16[3072,32]{0,1:T(8,128)(2,1)}, u32[]{:S(2)}) copy-start(bf16[3072,32]{0,1:T(8,128)(2,1)} %param.18) | copy-start | bytes 589828
  28.7 150.3 %all-gather.8.cloned.1.call-start = ((), (), s32[]{:S(2)}) async-start(), calls=%async_computation.2 | async-start | bytes 1671168 | tf_op jit(solution)/shard_map/all_gather | solution.py:101
  29.3 97.2 %copy-start.4 = (bf16[128,256]{1,0:T(8,128)(2,1)S(1)}, bf16[128,256]{1,0:T(8,128)(2,1)}, u32[]{:S(2)}) copy-start(bf16[128,256]{1,0:T(8,128)(2,1)} %param.12) | copy-start | bytes 196612
  31.3 369.2 %all-reduce.6.cloned.1.call-start = ((), (), s32[]{:S(2)}) async-start(), calls=%async_computation.3 | async-start | bytes 1572864
  126.4 16.8 %copy-start.2 = (bf16[128,256]{1,0:T(8,128)(2,1)S(1)}, bf16[128,256]{1,0:T(8,128)(2,1)}, u32[]{:S(2)}) copy-start(bf16[128,256]{1,0:T(8,128)(2,1)} %param.14) | copy-start | bytes 196612
  218.0 14.4 %collective-permute-start = (bf16[16,3072]{1,0:T(8,128)(2,1)S(1)}, bf16[16,3072]{1,0:T(8,128)(2,1)S(1)}, u32[]{:S(2)}, u32[]{:S(2)}) collective-permute-start(bf16[16,3072]{1,0:T(8,128)(2,1)S(1)} %fusion), channel_id=1, source_target_pairs={{0,32},{32,64},{64,96},{96,128},{128,160},{160,192},{192,224},{224... | collective-permute-start | bytes 294920
  220.6 11.8 %collective-permute-start.1 = (bf16[16,3072]{1,0:T(8,128)(2,1)S(1)}, bf16[16,3072]{1,0:T(8,128)(2,1)S(1)}, u32[]{:S(2)}, u32[]{:S(2)}) collective-permute-start(bf16[16,3072]{1,0:T(8,128)(2,1)S(1)} %fusion), channel_id=1, source_target_pairs={{0,64},{32,96},{64,128},{96,160},{128,192},{160,224},{192,256},{22... | collective-permute-start | bytes 294920
  222.8 10.3 %collective-permute-start.2 = (bf16[16,3072]{1,0:T(8,128)(2,1)S(1)}, bf16[16,3072]{1,0:T(8,128)(2,1)S(1)}, u32[]{:S(2)}, u32[]{:S(2)}) collective-permute-start(bf16[16,3072]{1,0:T(8,128)(2,1)S(1)} %fusion), channel_id=1, source_target_pairs={{0,96},{32,128},{64,160},{96,192},{128,224},{160,256},{192,288},{2... | collective-permute-start | bytes 294920
  226.8 5.6 %collective-permute-start.3 = (bf16[12,3072]{1,0:T(8,128)(2,1)S(1)}, bf16[12,3072]{1,0:T(8,128)(2,1)S(1)}, u32[]{:S(2)}, u32[]{:S(2)}) collective-permute-start(bf16[12,3072]{1,0:T(8,128)(2,1)S(1)} %slice.16), channel_id=1, source_target_pairs={{0,128},{32,160},{64,192},{96,224},{128,256},{160,288},{192,320},{... | collective-permute-start | bytes 221192
  232.4 0.6 copy-start.3
Sparse Core Ops, SparseCore 0:
  10.7 102.3 all-gather.5
  115.2 63.7 all-gather.7
  239.0 161.4 all-reduce.5
